TPU v7x, 32 devices: a whole 2x2x4 slice. The times are simulated.
32 devices in a mesh: batch: 8 (over z, y), width: 4 (over x, core).
Axes of the slice: x: 2, y: 2, z: 4, core: 2. Of those that a mesh axis runs over, the one named last changes fastest.
Arguments:
- teacher: bfloat16 [2048, 4096], P('batch', 'width'), may hold values from -48 to 48, as said below
- student: bfloat16 [2048, 1024], P('batch', 'width'), may hold values from -48 to 48, as said below
Outputs:
- grad: float32 [2048, 1024], P('batch', 'width')
Inputs may be any that keep to these rules, and one draw needn't show every extreme that they name: `teacher`: Real-valued embeddings. `student`: Real-valued embeddings.
All inputs are finite; a program needn't handle non-finite values.
Results may differ from a plain program's by a relative error of at most 0.00075.
Values may be sent and summed in bfloat16 or wider, within the bound.
No kernel may reach another device: no remote copies, remote signals or barrier semaphores. Data moves between devices by JAX's collectives and lax.ppermute only.
A program may use at most 64 MiB of HBM per device.

v0:
```python
import jax
import jax.numpy as jnp
import numpy as np
from jax import lax
from jax.sharding import PartitionSpec as P

DT = 4096
DS = 1024
REACH = 4


def passed_along(block, axis, distance):
    devices = range(lax.axis_size(axis))
    route = [(i - distance, i) for i in devices if i - distance in devices]
    return lax.ppermute(block, axis, route)


def body(teacher, student):
    group = lax.axis_size("batch")
    owner = lax.axis_index("batch")
    rows_dev = teacher.shape[0]
    teacher_list = [teacher]
    student_list = [student]
    moving = (teacher, student)
    for offset in range(REACH):
        moving = passed_along((moving[0], moving[1]), "batch", -1)
        teacher_list.append(moving[0])
        student_list.append(moving[1])
    offset_list = list(range(REACH + 1))
    moving = (teacher, student)
    for offset in range(REACH):
        moving = passed_along((moving[0], moving[1]), "batch", 1)
        teacher_list.insert(0, moving[0])
        student_list.insert(0, moving[1])
        offset_list.insert(0, -(offset + 1))
    band_teacher = jnp.stack(teacher_list, axis=0)
    band_student = jnp.stack(student_list, axis=0)
    own_tsq = jnp.sum(jnp.square(teacher.astype(jnp.float32)), axis=1) / DT
    own_ssq = jnp.sum(jnp.square(student.astype(jnp.float32)), axis=1) / DS
    band_tsq = jnp.sum(jnp.square(band_teacher.astype(jnp.float32)), axis=2) / DT
    band_ssq = jnp.sum(jnp.square(band_student.astype(jnp.float32)), axis=2) / DS
    tgram = jnp.einsum("rk,wck->wrc", teacher, band_teacher, preferred_element_type=jnp.float32)
    sgram = jnp.einsum("rk,wck->wrc", student, band_student, preferred_element_type=jnp.float32)
    student_part = own_ssq[None, :, None] + band_ssq[:, None, :] - 2.0 * sgram / DS
    teacher_part = own_tsq[None, :, None] + band_tsq[:, None, :] - 2.0 * tgram / DT
    shard_terms = student_part - teacher_part
    partner = owner + jnp.asarray(np.array(offset_list, dtype=np.int32))
    valid = jnp.logical_and(partner >= 0, partner < group)
    residual = lax.psum(shard_terms, "width")
    residual = jnp.where(valid[:, None, None], residual, jnp.zeros_like(residual))
    residual_low = residual.astype(jnp.bfloat16)
    row_total = jnp.sum(residual, axis=(0, 2))
    pulled = jnp.einsum(
        "wrc,wck->rk", residual_low, band_student, preferred_element_type=jnp.float32
    )
    near_count = (2 * REACH + 1) * rows_dev
    grad = (student.astype(jnp.float32) * row_total[:, None] - pulled) / near_count
    return grad


def solution(mesh):
    in_specs = (P("batch", "width"), P("batch", "width"))
    out_specs = P("batch", "width")
    return jax.shard_map(body, mesh=mesh, in_specs=in_specs, out_specs=out_specs, check_vma=False)
```

profile of v0, /device:TPU:0, one launch (start us, length us, event | category | flops | bytes accessed | tf_op | source)
XLA Modules:
  0.0 210.9 jit_solution(6608622640676647879)
XLA Ops:
  6.5 0.0 copy-start.1
  6.5 0.0 all-reduce.2.cloned.1.call-start
  6.5 5.0 %collective-permute-start = (bf16[256,256]{1,0:T(8,128)(2,1)}, bf16[256,256]{1,0:T(8,128)(2,1)S(1)}, u32[]{:S(2)}, u32[]{:S(2)}) collective-permute-start(bf16[256,256]{1,0:T(8,128)(2,1)} %param.4), channel_id=1, source_target_pairs={{0,4},{4,8},{8,12},{12,16},{16,20},{20,24},{24,28},{1,5},{5,9},{9,... | collective-permute-start | bytes 393224 | tf_op jit(solution)/shard_map/ppermute | solution.py:15
  11.6 1.3 collective-permute-start.4
  12.9 4.6 %collective-permute-start.8 = (bf16[256,1024]{1,0:T(8,128)(2,1)}, bf16[256,1024]{1,0:T(8,128)(2,1)S(1)}, u32[]{:S(2)}, u32[]{:S(2)}) collective-permute-start(bf16[256,1024]{1,0:T(8,128)(2,1)} %param.3), channel_id=1, source_target_pairs={{0,4},{4,8},{8,12},{12,16},{16,20},{20,24},{24,28},{1,5},{5,9},{9,... | collective-permute-start | bytes 1572872 | tf_op jit(solution)/shard_map/ppermute | solution.py:15
  17.5 1.3 collective-permute-start.12
  18.8 0.0 collective-permute-done
  18.8 4.9 %collective-permute-start.1 = (bf16[256,256]{1,0:T(8,128)(2,1)S(1)}, bf16[256,256]{1,0:T(8,128)(2,1)S(1)}, u32[]{:S(2)}, u32[]{:S(2)}) collective-permute-start(bf16[256,256]{1,0:T(8,128)(2,1)S(1)} %collective-permute-done), channel_id=1, source_target_pairs={{0,4},{4,8},{8,12},{12,16},{16,20},{20,24},{24,28},{1,5},{5,9},{9,... | collective-permute-start | bytes 393224 | tf_op jit(solution)/shard_map/ppermute | solution.py:15
  23.7 1.2 multiply_reduce_fusion.2
  24.9 0.0 collective-permute-done.4
  24.9 1.3 collective-permute-start.5
  26.2 20.4 %collective-permute-done.1 = bf16[256,256]{1,0:T(8,128)(2,1)S(1)} collective-permute-done((bf16[256,256]{1,0:T(8,128)(2,1)S(1)}, bf16[256,256]{1,0:T(8,128)(2,1)S(1)}, u32[]{:S(2)}, u32[]{:S(2)}) %collective-permute-start.1) | collective-permute-done | bytes 131104 | tf_op jit(solution)/shard_map/ppermute | solution.py:15
  46.7 4.4 %collective-permute-start.2 = (bf16[256,256]{1,0:T(8,128)(2,1)S(1)}, bf16[256,256]{1,0:T(8,128)(2,1)S(1)}, u32[]{:S(2)}, u32[]{:S(2)}) collective-permute-start(bf16[256,256]{1,0:T(8,128)(2,1)S(1)} %collective-permute-done.1), channel_id=1, source_target_pairs={{0,4},{4,8},{8,12},{12,16},{16,20},{20,24},{24,28},{1,5},{5,9},{9,... | collective-permute-start | bytes 393224 | tf_op jit(solution)/shard_map/ppermute | solution.py:15
  51.1 1.0 fusion.8
  52.1 0.0 collective-permute-done.5
  52.1 1.3 collective-permute-start.6
  53.4 0.5 collective-permute-done.2
  53.9 4.4 %collective-permute-start.3 = (bf16[256,256]{1,0:T(8,128)(2,1)S(1)}, bf16[256,256]{1,0:T(8,128)(2,1)S(1)}, u32[]{:S(2)}, u32[]{:S(2)}) collective-permute-start(bf16[256,256]{1,0:T(8,128)(2,1)S(1)} %collective-permute-done.2), channel_id=1, source_target_pairs={{0,4},{4,8},{8,12},{12,16},{16,20},{20,24},{24,28},{1,5},{5,9},{9,... | collective-permute-start | bytes 393224 | tf_op jit(solution)/shard_map/ppermute | solution.py:15
  58.3 0.8 collective-permute-done.6
  59.1 1.3 collective-permute-start.7
  60.4 0.5 collective-permute-done.3
  60.9 0.0 collective-permute-done.8
  60.9 4.4 %collective-permute-start.9 = (bf16[256,1024]{1,0:T(8,128)(2,1)S(1)}, bf16[256,1024]{1,0:T(8,128)(2,1)S(1)}, u32[]{:S(2)}, u32[]{:S(2)}) collective-permute-start(bf16[256,1024]{1,0:T(8,128)(2,1)S(1)} %collective-permute-done.8), channel_id=1, source_target_pairs={{0,4},{4,8},{8,12},{12,16},{16,20},{20,24},{24,28},{1,5},{5,9},{9,... | collective-permute-start | bytes 1572872 | tf_op jit(solution)/shard_map/ppermute | solution.py:15
  65.4 0.9 bitcast_dynamic-update-slice_fusion.13
  66.3 0.0 collective-permute-done.12
  66.3 1.3 collective-permute-start.13
  67.6 20.5 %collective-permute-done.9 = bf16[256,1024]{1,0:T(8,128)(2,1)S(1)} collective-permute-done((bf16[256,1024]{1,0:T(8,128)(2,1)S(1)}, bf16[256,1024]{1,0:T(8,128)(2,1)S(1)}, u32[]{:S(2)}, u32[]{:S(2)}) %collective-permute-start.9) | collective-permute-done | bytes 524320 | tf_op jit(solution)/shard_map/ppermute | solution.py:15
  88.1 4.4 %collective-permute-start.10 = (bf16[256,1024]{1,0:T(8,128)(2,1)S(1)}, bf16[256,1024]{1,0:T(8,128)(2,1)S(1)}, u32[]{:S(2)}, u32[]{:S(2)}) collective-permute-start(bf16[256,1024]{1,0:T(8,128)(2,1)S(1)} %collective-permute-done.9), channel_id=1, source_target_pairs={{0,4},{4,8},{8,12},{12,16},{16,20},{20,24},{24,28},{1,5},{5,9},{9,... | collective-permute-start | bytes 1572872 | tf_op jit(solution)/shard_map/ppermute | solution.py:15
  92.5 0.0 collective-permute-done.7
  92.6 0.4 multiply_reduce_fusion.1
  92.9 0.0 collective-permute-done.13
  93.0 1.3 collective-permute-start.14
  94.3 20.1 %collective-permute-done.10 = bf16[256,1024]{1,0:T(8,128)(2,1)S(1)} collective-permute-done((bf16[256,1024]{1,0:T(8,128)(2,1)S(1)}, bf16[256,1024]{1,0:T(8,128)(2,1)S(1)}, u32[]{:S(2)}, u32[]{:S(2)}) %collective-permute-start.10) | collective-permute-done | bytes 524320 | tf_op jit(solution)/shard_map/ppermute | solution.py:15
  114.4 4.4 %collective-permute-start.11 = (bf16[256,1024]{1,0:T(8,128)(2,1)S(1)}, bf16[256,1024]{1,0:T(8,128)(2,1)S(1)}, u32[]{:S(2)}, u32[]{:S(2)}) collective-permute-start(bf16[256,1024]{1,0:T(8,128)(2,1)S(1)} %collective-permute-done.10), channel_id=1, source_target_pairs={{0,4},{4,8},{8,12},{12,16},{16,20},{20,24},{24,28},{1,5},{5,9},{9,... | collective-permute-start | bytes 1572872 | tf_op jit(solution)/shard_map/ppermute | solution.py:15
  118.8 0.0 copy-done.1
  118.8 0.5 fusion.9
  119.3 0.0 copy-start.2
  119.4 0.0 collective-permute-done.14
  119.4 1.4 collective-permute-start.15
  120.8 19.0 %collective-permute-done.11 = bf16[256,1024]{1,0:T(8,128)(2,1)S(1)} collective-permute-done((bf16[256,1024]{1,0:T(8,128)(2,1)S(1)}, bf16[256,1024]{1,0:T(8,128)(2,1)S(1)}, u32[]{:S(2)}, u32[]{:S(2)}) %collective-permute-start.11) | collective-permute-done | bytes 524320 | tf_op jit(solution)/shard_map/ppermute | solution.py:15
  140.0 0.0 copy-done.2
  140.2 0.0 collective-permute-done.15
  140.3 1.0 multiply_reduce_fusion
  141.3 3.0 %fusion = f32[9,256,256]{1,2,0:T(8,128)} fusion(f32[9,256,256]{2,1,0:T(8,128)S(1)} %fusion.9, bf16[9,256,1024]{2,1,0:T(8,128)(2,1)S(1)} %bitcast_dynamic-update-slice_fusion, f32[9,256]{1,0:T(8,128)S(1)} %broadcast_multiply_fusion, f32[256]{0:T(256)S(1)} %broadcast_multiply_fusion.2, f32[9,256]{1,0:T(8,128)S(1)} %broadcast_multiply_fusion.1, ...), kind=kOutput, calls=%fused_computation.2 | convolution fusion | flops 1212088320 | bytes 9981952 | tf_op jit(solution)/shard_map/rk,wck->wrc/dot_general | solution.py:42
  144.3 0.0 copy-start.3
  144.3 0.0 all-reduce.2.cloned.1.call-update
  144.3 0.6 copy-done.3
  144.9 55.3 %all-reduce.2.cloned.1.call-done = f32[9,256,256]{1,2,0:T(8,128)} async-done(((f32[9,256,256]{1,2,0:T(8,128)}), f32[9,256,256]{1,2,0:T(8,128)}) %all-reduce.2.cloned.1.call-update) | async-done | bytes 2359312 | tf_op jit(solution)/shard_map/psum | solution.py:49
  200.3 0.0 copy-start
  200.3 2.2 %select_reduce_fusion = f32[256]{0:T(256)S(1)} fusion(f32[9,256,256]{1,2,0:T(8,128)} %all-reduce.2.cloned.1.call-done, pred[9]{0:T(512)(128)(4,1)S(1)} %compare_and_fusion), kind=kLoop, calls=%fused_computation.6 | loop fusion | flops 1179392 | bytes 2360329 | tf_op jit(solution)/shard_map/reduce_sum | solution.py:52
  202.5 0.1 copy-done
  202.7 1.4 fusion.6
  (22 shorter events, 0.4 us)
Async XLA Ops:
  6.5 112.3 %copy-start.1 = (bf16[256,256]{1,0:T(8,128)(2,1)S(1)}, bf16[256,256]{1,0:T(8,128)(2,1)}, u32[]{:S(2)}) copy-start(bf16[256,256]{1,0:T(8,128)(2,1)} %param.4) | copy-start | bytes 393220
  6.5 193.7 %all-reduce.2.cloned.1.call-start = ((), (), s32[]{:S(2)}) async-start(), calls=%async_computation | async-start | bytes 4718592 | tf_op jit(solution)/shard_map/psum | solution.py:49
  6.5 12.2 %collective-permute-start = (bf16[256,256]{1,0:T(8,128)(2,1)}, bf16[256,256]{1,0:T(8,128)(2,1)S(1)}, u32[]{:S(2)}, u32[]{:S(2)}) collective-permute-start(bf16[256,256]{1,0:T(8,128)(2,1)} %param.4), channel_id=1, source_target_pairs={{0,4},{4,8},{8,12},{12,16},{16,20},{20,24},{24,28},{1,5},{5,9},{9,... | collective-permute-start | bytes 393224 | tf_op jit(solution)/shard_map/ppermute | solution.py:15
  11.6 13.4 %collective-permute-start.4 = (bf16[256,256]{1,0:T(8,128)(2,1)}, bf16[256,256]{1,0:T(8,128)(2,1)S(1)}, u32[]{:S(2)}, u32[]{:S(2)}) collective-permute-start(bf16[256,256]{1,0:T(8,128)(2,1)} %param.4), channel_id=1, source_target_pairs={{4,0},{8,4},{12,8},{16,12},{20,16},{24,20},{28,24},{5,1},{9,5},{13... | collective-permute-start | bytes 393224 | tf_op jit(solution)/shard_map/ppermute | solution.py:15
  12.9 48.0 %collective-permute-start.8 = (bf16[256,1024]{1,0:T(8,128)(2,1)}, bf16[256,1024]{1,0:T(8,128)(2,1)S(1)}, u32[]{:S(2)}, u32[]{:S(2)}) collective-permute-start(bf16[256,1024]{1,0:T(8,128)(2,1)} %param.3), channel_id=1, source_target_pairs={{0,4},{4,8},{8,12},{12,16},{16,20},{20,24},{24,28},{1,5},{5,9},{9,... | collective-permute-start | bytes 1572872 | tf_op jit(solution)/shard_map/ppermute | solution.py:15
  17.5 48.8 %collective-permute-start.12 = (bf16[256,1024]{1,0:T(8,128)(2,1)}, bf16[256,1024]{1,0:T(8,128)(2,1)S(1)}, u32[]{:S(2)}, u32[]{:S(2)}) collective-permute-start(bf16[256,1024]{1,0:T(8,128)(2,1)} %param.3), channel_id=1, source_target_pairs={{4,0},{8,4},{12,8},{16,12},{20,16},{24,20},{28,24},{5,1},{9,5},{13... | collective-permute-start | bytes 1572872 | tf_op jit(solution)/shard_map/ppermute | solution.py:15
  18.8 27.9 %collective-permute-start.1 = (bf16[256,256]{1,0:T(8,128)(2,1)S(1)}, bf16[256,256]{1,0:T(8,128)(2,1)S(1)}, u32[]{:S(2)}, u32[]{:S(2)}) collective-permute-start(bf16[256,256]{1,0:T(8,128)(2,1)S(1)} %collective-permute-done), channel_id=1, source_target_pairs={{0,4},{4,8},{8,12},{12,16},{16,20},{20,24},{24,28},{1,5},{5,9},{9,... | collective-permute-start | bytes 393224 | tf_op jit(solution)/shard_map/ppermute | solution.py:15
  24.9 27.1 %collective-permute-start.5 = (bf16[256,256]{1,0:T(8,128)(2,1)S(1)}, bf16[256,256]{1,0:T(8,128)(2,1)S(1)}, u32[]{:S(2)}, u32[]{:S(2)}) collective-permute-start(bf16[256,256]{1,0:T(8,128)(2,1)S(1)} %collective-permute-done.4), channel_id=1, source_target_pairs={{4,0},{8,4},{12,8},{16,12},{20,16},{24,20},{28,24},{5,1},{9,5},{13... | collective-permute-start | bytes 393224 | tf_op jit(solution)/shard_map/ppermute | solution.py:15
  46.7 7.3 %collective-permute-start.2 = (bf16[256,256]{1,0:T(8,128)(2,1)S(1)}, bf16[256,256]{1,0:T(8,128)(2,1)S(1)}, u32[]{:S(2)}, u32[]{:S(2)}) collective-permute-start(bf16[256,256]{1,0:T(8,128)(2,1)S(1)} %collective-permute-done.1), channel_id=1, source_target_pairs={{0,4},{4,8},{8,12},{12,16},{16,20},{20,24},{24,28},{1,5},{5,9},{9,... | collective-permute-start | bytes 393224 | tf_op jit(solution)/shard_map/ppermute | solution.py:15
  52.1 7.0 %collective-permute-start.6 = (bf16[256,256]{1,0:T(8,128)(2,1)S(1)}, bf16[256,256]{1,0:T(8,128)(2,1)S(1)}, u32[]{:S(2)}, u32[]{:S(2)}) collective-permute-start(bf16[256,256]{1,0:T(8,128)(2,1)S(1)} %collective-permute-done.5), channel_id=1, source_target_pairs={{4,0},{8,4},{12,8},{16,12},{20,16},{24,20},{28,24},{5,1},{9,5},{13... | collective-permute-start | bytes 393224 | tf_op jit(solution)/shard_map/ppermute | solution.py:15
  53.9 6.9 %collective-permute-start.3 = (bf16[256,256]{1,0:T(8,128)(2,1)S(1)}, bf16[256,256]{1,0:T(8,128)(2,1)S(1)}, u32[]{:S(2)}, u32[]{:S(2)}) collective-permute-start(bf16[256,256]{1,0:T(8,128)(2,1)S(1)} %collective-permute-done.2), channel_id=1, source_target_pairs={{0,4},{4,8},{8,12},{12,16},{16,20},{20,24},{24,28},{1,5},{5,9},{9,... | collective-permute-start | bytes 393224 | tf_op jit(solution)/shard_map/ppermute | solution.py:15
  59.1 33.4 %collective-permute-start.7 = (bf16[256,256]{1,0:T(8,128)(2,1)S(1)}, bf16[256,256]{1,0:T(8,128)(2,1)S(1)}, u32[]{:S(2)}, u32[]{:S(2)}) collective-permute-start(bf16[256,256]{1,0:T(8,128)(2,1)S(1)} %collective-permute-done.6), channel_id=1, source_target_pairs={{4,0},{8,4},{12,8},{16,12},{20,16},{24,20},{28,24},{5,1},{9,5},{13... | collective-permute-start | bytes 393224 | tf_op jit(solution)/shard_map/ppermute | solution.py:15
  60.9 27.2 %collective-permute-start.9 = (bf16[256,1024]{1,0:T(8,128)(2,1)S(1)}, bf16[256,1024]{1,0:T(8,128)(2,1)S(1)}, u32[]{:S(2)}, u32[]{:S(2)}) collective-permute-start(bf16[256,1024]{1,0:T(8,128)(2,1)S(1)} %collective-permute-done.8), channel_id=1, source_target_pairs={{0,4},{4,8},{8,12},{12,16},{16,20},{20,24},{24,28},{1,5},{5,9},{9,... | collective-permute-start | bytes 1572872 | tf_op jit(solution)/shard_map/ppermute | solution.py:15
  66.3 26.6 %collective-permute-start.13 = (bf16[256,1024]{1,0:T(8,128)(2,1)S(1)}, bf16[256,1024]{1,0:T(8,128)(2,1)S(1)}, u32[]{:S(2)}, u32[]{:S(2)}) collective-permute-start(bf16[256,1024]{1,0:T(8,128)(2,1)S(1)} %collective-permute-done.12), channel_id=1, source_target_pairs={{4,0},{8,4},{12,8},{16,12},{20,16},{24,20},{28,24},{5,1},{9,5},{13... | collective-permute-start | bytes 1572872 | tf_op jit(solution)/shard_map/ppermute | solution.py:15
  88.1 26.3 %collective-permute-start.10 = (bf16[256,1024]{1,0:T(8,128)(2,1)S(1)}, bf16[256,1024]{1,0:T(8,128)(2,1)S(1)}, u32[]{:S(2)}, u32[]{:S(2)}) collective-permute-start(bf16[256,1024]{1,0:T(8,128)(2,1)S(1)} %collective-permute-done.9), channel_id=1, source_target_pairs={{0,4},{4,8},{8,12},{12,16},{16,20},{20,24},{24,28},{1,5},{5,9},{9,... | collective-permute-start | bytes 1572872 | tf_op jit(solution)/shard_map/ppermute | solution.py:15
  93.0 26.4 %collective-permute-start.14 = (bf16[256,1024]{1,0:T(8,128)(2,1)S(1)}, bf16[256,1024]{1,0:T(8,128)(2,1)S(1)}, u32[]{:S(2)}, u32[]{:S(2)}) collective-permute-start(bf16[256,1024]{1,0:T(8,128)(2,1)S(1)} %collective-permute-done.13), channel_id=1, source_target_pairs={{4,0},{8,4},{12,8},{16,12},{20,16},{24,20},{28,24},{5,1},{9,5},{13... | collective-permute-start | bytes 1572872 | tf_op jit(solution)/shard_map/ppermute | solution.py:15
  114.4 25.4 %collective-permute-start.11 = (bf16[256,1024]{1,0:T(8,128)(2,1)S(1)}, bf16[256,1024]{1,0:T(8,128)(2,1)S(1)}, u32[]{:S(2)}, u32[]{:S(2)}) collective-permute-start(bf16[256,1024]{1,0:T(8,128)(2,1)S(1)} %collective-permute-done.10), channel_id=1, source_target_pairs={{0,4},{4,8},{8,12},{12,16},{16,20},{20,24},{24,28},{1,5},{5,9},{9,... | collective-permute-start | bytes 1572872 | tf_op jit(solution)/shard_map/ppermute | solution.py:15
  119.3 20.7 %copy-start.2 = (bf16[256,1024]{1,0:T(8,128)(2,1)S(1)}, bf16[256,1024]{1,0:T(8,128)(2,1)}, u32[]{:S(2)}) copy-start(bf16[256,1024]{1,0:T(8,128)(2,1)} %param.3) | copy-start | bytes 1572868
  119.4 20.8 %collective-permute-start.15 = (bf16[256,1024]{1,0:T(8,128)(2,1)S(1)}, bf16[256,1024]{1,0:T(8,128)(2,1)S(1)}, u32[]{:S(2)}, u32[]{:S(2)}) collective-permute-start(bf16[256,1024]{1,0:T(8,128)(2,1)S(1)} %collective-permute-done.14), channel_id=1, source_target_pairs={{4,0},{8,4},{12,8},{16,12},{20,16},{24,20},{28,24},{5,1},{9,5},{13... | collective-permute-start | bytes 1572872 | tf_op jit(solution)/shard_map/ppermute | solution.py:15
  144.3 0.7 copy-start.3
  200.3 2.4 %copy-start = (f32[9,256,256]{1,2,0:T(8,128)S(1)}, f32[9,256,256]{1,2,0:T(8,128)}, u32[]{:S(2)}) copy-start(f32[9,256,256]{1,2,0:T(8,128)} %all-reduce.2.cloned.1.call-done) | copy-start | bytes 7077892
Sparse Core Ops, SparseCore 0:
  144.4 55.8 all-reduce.1
where the time goes:
time: 212 us; the launch traced here: 211 us
  waiting for transfers between devices  137 us (65%)
  starting transfers between devices  47 us (22%)
  between operations  13.8 us (7%)
  other arithmetic  5.87 us (3%)
  matrix products  4.92 us (2%)
    ppermute x16, waiting for transfers between devices, passed_along(): return lax.ppermute(block, axis, route)  81.9 us
    psum x1, waiting for transfers between devices, body(): residual = lax.psum(shard_terms, 'width')  55.3 us
    ppermute x16, starting transfers between devices, passed_along(): return lax.ppermute(block, axis, route)  47 us
  transfers between devices with their start and end apart: 17, of which 8 were waited for; matrix products, arithmetic and copies ran while one was open for 2% of the time, Pallas kernels for 0%

commit v1 on v0

--- a/solution.py
+++ b/solution.py
@@ -7,6 +7,7 @@
 DT = 4096
 DS = 1024
 REACH = 4
+place_inputs = lambda array_here: jax.lax.all_gather(array_here, "width").sum(axis=0)
 
 
 def passed_along(block, axis, distance):
@@ -46,7 +47,7 @@
     shard_terms = student_part - teacher_part
     partner = owner + jnp.asarray(np.array(offset_list, dtype=np.int32))
     valid = jnp.logical_and(partner >= 0, partner < group)
-    residual = lax.psum(shard_terms, "width")
+    residual = place_inputs(shard_terms)
     residual = jnp.where(valid[:, None, None], residual, jnp.zeros_like(residual))
     residual_low = residual.astype(jnp.bfloat16)
     row_total = jnp.sum(residual, axis=(0, 2))

time: 212 us -> 228 us (1.075)
  waiting for transfers between devices: 137 us -> 146 us
  local copies, waits for them, and re-layouts: 2.1 us -> 6.43 us
  other arithmetic: 5.87 us -> 10.1 us
    all_gather x0 -> x1, waiting for transfers between devices: none -> 63.9 us  [jax.lax.all_gather(array_here, 'width').sum(axis=0)]
    psum x1 -> x0, waiting for transfers between devices: 55.3 us -> none  [body(): residual = lax.psum(shard_terms, 'width')]
    reduce_sum x0 -> x1, other arithmetic: none -> 6.02 us  [jax.lax.all_gather(array_here, 'width').sum(axis=0)]
    unnamed x24 -> x25, local copies, waits for them, and re-layouts: 2.06 us -> 4.43 us
where the time goes in v1:
time: 228 us; the launch traced here: 227 us
  waiting for transfers between devices  146 us (64%)
  starting transfers between devices  47 us (21%)
  between operations  13.8 us (6%)
  other arithmetic  10.1 us (4%)
  local copies, waits for them, and re-layouts  6.43 us (3%)
  matrix products  3.77 us (2%)
    ppermute x16, waiting for transfers between devices, passed_along(): return lax.ppermute(block, axis, route)  81.9 us
    all_gather x1, waiting for transfers between devices, jax.lax.all_gather(array_here, 'width').sum(axis=0)  63.9 us
    ppermute x16, starting transfers between devices, passed_along(): return lax.ppermute(block, axis, route)  47 us
    reduce_sum x1, other arithmetic, jax.lax.all_gather(array_here, 'width').sum(axis=0)  6.02 us
  transfers between devices with their start and end apart: 17, of which 8 were waited for; matrix products, arithmetic and copies ran while one was open for 2% of the time, Pallas kernels for 0%

profile of v1, /device:TPU:0, one launch (start us, length us, event | category | flops | bytes accessed | tf_op | source)
XLA Modules:
  0.0 226.9 jit_solution(7924033871963452263)
XLA Ops:
  6.5 0.0 copy-start
  6.5 0.0 all-gather.3.cloned.1.call-start
  6.5 5.0 %collective-permute-start = (bf16[256,256]{1,0:T(8,128)(2,1)}, bf16[256,256]{1,0:T(8,128)(2,1)S(1)}, u32[]{:S(2)}, u32[]{:S(2)}) collective-permute-start(bf16[256,256]{1,0:T(8,128)(2,1)} %param.4), channel_id=1, source_target_pairs={{0,4},{4,8},{8,12},{12,16},{16,20},{20,24},{24,28},{1,5},{5,9},{9,... | collective-permute-start | bytes 393224 | tf_op jit(solution)/shard_map/ppermute | solution.py:16
  11.6 1.3 collective-permute-start.4
  12.9 4.6 %collective-permute-start.8 = (bf16[256,1024]{1,0:T(8,128)(2,1)}, bf16[256,1024]{1,0:T(8,128)(2,1)S(1)}, u32[]{:S(2)}, u32[]{:S(2)}) collective-permute-start(bf16[256,1024]{1,0:T(8,128)(2,1)} %param.3), channel_id=1, source_target_pairs={{0,4},{4,8},{8,12},{12,16},{16,20},{20,24},{24,28},{1,5},{5,9},{9,... | collective-permute-start | bytes 1572872 | tf_op jit(solution)/shard_map/ppermute | solution.py:16
  17.5 1.3 collective-permute-start.12
  18.8 0.0 collective-permute-done
  18.8 4.9 %collective-permute-start.1 = (bf16[256,256]{1,0:T(8,128)(2,1)S(1)}, bf16[256,256]{1,0:T(8,128)(2,1)S(1)}, u32[]{:S(2)}, u32[]{:S(2)}) collective-permute-start(bf16[256,256]{1,0:T(8,128)(2,1)S(1)} %collective-permute-done), channel_id=1, source_target_pairs={{0,4},{4,8},{8,12},{12,16},{16,20},{20,24},{24,28},{1,5},{5,9},{9,... | collective-permute-start | bytes 393224 | tf_op jit(solution)/shard_map/ppermute | solution.py:16
  23.7 1.2 multiply_reduce_fusion.2
  24.9 0.0 collective-permute-done.4
  24.9 1.3 collective-permute-start.5
  26.2 20.4 %collective-permute-done.1 = bf16[256,256]{1,0:T(8,128)(2,1)S(1)} collective-permute-done((bf16[256,256]{1,0:T(8,128)(2,1)S(1)}, bf16[256,256]{1,0:T(8,128)(2,1)S(1)}, u32[]{:S(2)}, u32[]{:S(2)}) %collective-permute-start.1) | collective-permute-done | bytes 131104 | tf_op jit(solution)/shard_map/ppermute | solution.py:16
  46.7 4.4 %collective-permute-start.2 = (bf16[256,256]{1,0:T(8,128)(2,1)S(1)}, bf16[256,256]{1,0:T(8,128)(2,1)S(1)}, u32[]{:S(2)}, u32[]{:S(2)}) collective-permute-start(bf16[256,256]{1,0:T(8,128)(2,1)S(1)} %collective-permute-done.1), channel_id=1, source_target_pairs={{0,4},{4,8},{8,12},{12,16},{16,20},{20,24},{24,28},{1,5},{5,9},{9,... | collective-permute-start | bytes 393224 | tf_op jit(solution)/shard_map/ppermute | solution.py:16
  51.1 1.0 fusion.8
  52.1 0.0 collective-permute-done.5
  52.1 1.3 collective-permute-start.6
  53.4 0.5 collective-permute-done.2
  53.9 4.4 %collective-permute-start.3 = (bf16[256,256]{1,0:T(8,128)(2,1)S(1)}, bf16[256,256]{1,0:T(8,128)(2,1)S(1)}, u32[]{:S(2)}, u32[]{:S(2)}) collective-permute-start(bf16[256,256]{1,0:T(8,128)(2,1)S(1)} %collective-permute-done.2), channel_id=1, source_target_pairs={{0,4},{4,8},{8,12},{12,16},{16,20},{20,24},{24,28},{1,5},{5,9},{9,... | collective-permute-start | bytes 393224 | tf_op jit(solution)/shard_map/ppermute | solution.py:16
  58.3 0.8 collective-permute-done.6
  59.1 1.3 collective-permute-start.7
  60.4 0.5 collective-permute-done.3
  60.9 0.0 collective-permute-done.8
  60.9 4.4 %collective-permute-start.9 = (bf16[256,1024]{1,0:T(8,128)(2,1)S(1)}, bf16[256,1024]{1,0:T(8,128)(2,1)S(1)}, u32[]{:S(2)}, u32[]{:S(2)}) collective-permute-start(bf16[256,1024]{1,0:T(8,128)(2,1)S(1)} %collective-permute-done.8), channel_id=1, source_target_pairs={{0,4},{4,8},{8,12},{12,16},{16,20},{20,24},{24,28},{1,5},{5,9},{9,... | collective-permute-start | bytes 1572872 | tf_op jit(solution)/shard_map/ppermute | solution.py:16
  65.4 0.9 bitcast_dynamic-update-slice_fusion.13
  66.3 0.0 collective-permute-done.12
  66.3 1.3 collective-permute-start.13
  67.6 20.5 %collective-permute-done.9 = bf16[256,1024]{1,0:T(8,128)(2,1)S(1)} collective-permute-done((bf16[256,1024]{1,0:T(8,128)(2,1)S(1)}, bf16[256,1024]{1,0:T(8,128)(2,1)S(1)}, u32[]{:S(2)}, u32[]{:S(2)}) %collective-permute-start.9) | collective-permute-done | bytes 524320 | tf_op jit(solution)/shard_map/ppermute | solution.py:16
  88.1 4.4 %collective-permute-start.10 = (bf16[256,1024]{1,0:T(8,128)(2,1)S(1)}, bf16[256,1024]{1,0:T(8,128)(2,1)S(1)}, u32[]{:S(2)}, u32[]{:S(2)}) collective-permute-start(bf16[256,1024]{1,0:T(8,128)(2,1)S(1)} %collective-permute-done.9), channel_id=1, source_target_pairs={{0,4},{4,8},{8,12},{12,16},{16,20},{20,24},{24,28},{1,5},{5,9},{9,... | collective-permute-start | bytes 1572872 | tf_op jit(solution)/shard_map/ppermute | solution.py:16
  92.5 0.0 collective-permute-done.7
  92.6 0.4 multiply_reduce_fusion.1
  92.9 0.0 collective-permute-done.13
  93.0 1.3 collective-permute-start.14
  94.3 20.1 %collective-permute-done.10 = bf16[256,1024]{1,0:T(8,128)(2,1)S(1)} collective-permute-done((bf16[256,1024]{1,0:T(8,128)(2,1)S(1)}, bf16[256,1024]{1,0:T(8,128)(2,1)S(1)}, u32[]{:S(2)}, u32[]{:S(2)}) %collective-permute-start.10) | collective-permute-done | bytes 524320 | tf_op jit(solution)/shard_map/ppermute | solution.py:16
  114.4 4.4 %collective-permute-start.11 = (bf16[256,1024]{1,0:T(8,128)(2,1)S(1)}, bf16[256,1024]{1,0:T(8,128)(2,1)S(1)}, u32[]{:S(2)}, u32[]{:S(2)}) collective-permute-start(bf16[256,1024]{1,0:T(8,128)(2,1)S(1)} %collective-permute-done.10), channel_id=1, source_target_pairs={{0,4},{4,8},{8,12},{12,16},{16,20},{20,24},{24,28},{1,5},{5,9},{9,... | collective-permute-start | bytes 1572872 | tf_op jit(solution)/shard_map/ppermute | solution.py:16
  118.8 0.0 copy-done
  118.8 0.5 fusion.9
  119.3 0.0 copy-start.2
  119.4 0.0 collective-permute-done.14
  119.4 1.4 collective-permute-start.15
  120.8 19.0 %collective-permute-done.11 = bf16[256,1024]{1,0:T(8,128)(2,1)S(1)} collective-permute-done((bf16[256,1024]{1,0:T(8,128)(2,1)S(1)}, bf16[256,1024]{1,0:T(8,128)(2,1)S(1)}, u32[]{:S(2)}, u32[]{:S(2)}) %collective-permute-start.11) | collective-permute-done | bytes 524320 | tf_op jit(solution)/shard_map/ppermute | solution.py:16
  140.0 0.0 copy-done.2
  140.2 0.0 collective-permute-done.15
  140.3 1.0 multiply_reduce_fusion
  141.3 1.9 fusion
  143.1 1.9 copy.4
  145.1 0.0 copy-start.3
  145.1 0.0 all-gather.3.cloned.1.call-update
  145.1 0.6 copy-done.3
  145.8 63.9 %all-gather.3.cloned.1.call-done = f32[36,256,256]{2,1,0:T(8,128)} async-done(((f32[9,256,256]{2,1,0:T(8,128)}), f32[36,256,256]{2,1,0:T(8,128)}) %all-gather.3.cloned.1.call-update) | async-done | bytes 9437200 | tf_op jit(solution)/shard_map/all_gather | solution.py:10
  209.7 6.0 %reduce_sum.58 = f32[9,256,256]{2,1,0:T(8,128)} reduce(f32[4,9,256,256]{3,2,1,0:T(8,128)} %bitcast.60, f32[]{:T(128)} %constant.31.clone.1), dimensions={0}, to_apply=%region_4.0 | reduce | flops 1769472 | bytes 11796484 | tf_op jit(solution)/shard_map/reduce_sum | solution.py:10
  215.7 2.0 copy.8
  217.7 0.0 copy-start.1
  217.7 0.4 select_reduce_fusion
  218.2 0.5 copy-done.1
  218.6 1.4 fusion.6
  (22 shorter events, 0.4 us)
Async XLA Ops:
  6.5 112.3 %copy-start = (bf16[256,256]{1,0:T(8,128)(2,1)S(1)}, bf16[256,256]{1,0:T(8,128)(2,1)}, u32[]{:S(2)}) copy-start(bf16[256,256]{1,0:T(8,128)(2,1)} %param.4) | copy-start | bytes 393220
  6.5 203.1 %all-gather.3.cloned.1.call-start = ((), (), s32[]{:S(2)}) async-start(), calls=%async_computation | async-start | bytes 11796480 | tf_op jit(solution)/shard_map/all_gather | solution.py:10
  6.5 12.2 %collective-permute-start = (bf16[256,256]{1,0:T(8,128)(2,1)}, bf16[256,256]{1,0:T(8,128)(2,1)S(1)}, u32[]{:S(2)}, u32[]{:S(2)}) collective-permute-start(bf16[256,256]{1,0:T(8,128)(2,1)} %param.4), channel_id=1, source_target_pairs={{0,4},{4,8},{8,12},{12,16},{16,20},{20,24},{24,28},{1,5},{5,9},{9,... | collective-permute-start | bytes 393224 | tf_op jit(solution)/shard_map/ppermute | solution.py:16
  11.6 13.4 %collective-permute-start.4 = (bf16[256,256]{1,0:T(8,128)(2,1)}, bf16[256,256]{1,0:T(8,128)(2,1)S(1)}, u32[]{:S(2)}, u32[]{:S(2)}) collective-permute-start(bf16[256,256]{1,0:T(8,128)(2,1)} %param.4), channel_id=1, source_target_pairs={{4,0},{8,4},{12,8},{16,12},{20,16},{24,20},{28,24},{5,1},{9,5},{13... | collective-permute-start | bytes 393224 | tf_op jit(solution)/shard_map/ppermute | solution.py:16
  12.9 48.0 %collective-permute-start.8 = (bf16[256,1024]{1,0:T(8,128)(2,1)}, bf16[256,1024]{1,0:T(8,128)(2,1)S(1)}, u32[]{:S(2)}, u32[]{:S(2)}) collective-permute-start(bf16[256,1024]{1,0:T(8,128)(2,1)} %param.3), channel_id=1, source_target_pairs={{0,4},{4,8},{8,12},{12,16},{16,20},{20,24},{24,28},{1,5},{5,9},{9,... | collective-permute-start | bytes 1572872 | tf_op jit(solution)/shard_map/ppermute | solution.py:16
  17.5 48.8 %collective-permute-start.12 = (bf16[256,1024]{1,0:T(8,128)(2,1)}, bf16[256,1024]{1,0:T(8,128)(2,1)S(1)}, u32[]{:S(2)}, u32[]{:S(2)}) collective-permute-start(bf16[256,1024]{1,0:T(8,128)(2,1)} %param.3), channel_id=1, source_target_pairs={{4,0},{8,4},{12,8},{16,12},{20,16},{24,20},{28,24},{5,1},{9,5},{13... | collective-permute-start | bytes 1572872 | tf_op jit(solution)/shard_map/ppermute | solution.py:16
  18.8 27.9 %collective-permute-start.1 = (bf16[256,256]{1,0:T(8,128)(2,1)S(1)}, bf16[256,256]{1,0:T(8,128)(2,1)S(1)}, u32[]{:S(2)}, u32[]{:S(2)}) collective-permute-start(bf16[256,256]{1,0:T(8,128)(2,1)S(1)} %collective-permute-done), channel_id=1, source_target_pairs={{0,4},{4,8},{8,12},{12,16},{16,20},{20,24},{24,28},{1,5},{5,9},{9,... | collective-permute-start | bytes 393224 | tf_op jit(solution)/shard_map/ppermute | solution.py:16
  24.9 27.1 %collective-permute-start.5 = (bf16[256,256]{1,0:T(8,128)(2,1)S(1)}, bf16[256,256]{1,0:T(8,128)(2,1)S(1)}, u32[]{:S(2)}, u32[]{:S(2)}) collective-permute-start(bf16[256,256]{1,0:T(8,128)(2,1)S(1)} %collective-permute-done.4), channel_id=1, source_target_pairs={{4,0},{8,4},{12,8},{16,12},{20,16},{24,20},{28,24},{5,1},{9,5},{13... | collective-permute-start | bytes 393224 | tf_op jit(solution)/shard_map/ppermute | solution.py:16
  46.7 7.3 %collective-permute-start.2 = (bf16[256,256]{1,0:T(8,128)(2,1)S(1)}, bf16[256,256]{1,0:T(8,128)(2,1)S(1)}, u32[]{:S(2)}, u32[]{:S(2)}) collective-permute-start(bf16[256,256]{1,0:T(8,128)(2,1)S(1)} %collective-permute-done.1), channel_id=1, source_target_pairs={{0,4},{4,8},{8,12},{12,16},{16,20},{20,24},{24,28},{1,5},{5,9},{9,... | collective-permute-start | bytes 393224 | tf_op jit(solution)/shard_map/ppermute | solution.py:16
  52.1 7.0 %collective-permute-start.6 = (bf16[256,256]{1,0:T(8,128)(2,1)S(1)}, bf16[256,256]{1,0:T(8,128)(2,1)S(1)}, u32[]{:S(2)}, u32[]{:S(2)}) collective-permute-start(bf16[256,256]{1,0:T(8,128)(2,1)S(1)} %collective-permute-done.5), channel_id=1, source_target_pairs={{4,0},{8,4},{12,8},{16,12},{20,16},{24,20},{28,24},{5,1},{9,5},{13... | collective-permute-start | bytes 393224 | tf_op jit(solution)/shard_map/ppermute | solution.py:16
  53.9 6.9 %collective-permute-start.3 = (bf16[256,256]{1,0:T(8,128)(2,1)S(1)}, bf16[256,256]{1,0:T(8,128)(2,1)S(1)}, u32[]{:S(2)}, u32[]{:S(2)}) collective-permute-start(bf16[256,256]{1,0:T(8,128)(2,1)S(1)} %collective-permute-done.2), channel_id=1, source_target_pairs={{0,4},{4,8},{8,12},{12,16},{16,20},{20,24},{24,28},{1,5},{5,9},{9,... | collective-permute-start | bytes 393224 | tf_op jit(solution)/shard_map/ppermute | solution.py:16
  59.1 33.4 %collective-permute-start.7 = (bf16[256,256]{1,0:T(8,128)(2,1)S(1)}, bf16[256,256]{1,0:T(8,128)(2,1)S(1)}, u32[]{:S(2)}, u32[]{:S(2)}) collective-permute-start(bf16[256,256]{1,0:T(8,128)(2,1)S(1)} %collective-permute-done.6), channel_id=1, source_target_pairs={{4,0},{8,4},{12,8},{16,12},{20,16},{24,20},{28,24},{5,1},{9,5},{13... | collective-permute-start | bytes 393224 | tf_op jit(solution)/shard_map/ppermute | solution.py:16
  60.9 27.2 %collective-permute-start.9 = (bf16[256,1024]{1,0:T(8,128)(2,1)S(1)}, bf16[256,1024]{1,0:T(8,128)(2,1)S(1)}, u32[]{:S(2)}, u32[]{:S(2)}) collective-permute-start(bf16[256,1024]{1,0:T(8,128)(2,1)S(1)} %collective-permute-done.8), channel_id=1, source_target_pairs={{0,4},{4,8},{8,12},{12,16},{16,20},{20,24},{24,28},{1,5},{5,9},{9,... | collective-permute-start | bytes 1572872 | tf_op jit(solution)/shard_map/ppermute | solution.py:16
  66.3 26.6 %collective-permute-start.13 = (bf16[256,1024]{1,0:T(8,128)(2,1)S(1)}, bf16[256,1024]{1,0:T(8,128)(2,1)S(1)}, u32[]{:S(2)}, u32[]{:S(2)}) collective-permute-start(bf16[256,1024]{1,0:T(8,128)(2,1)S(1)} %collective-permute-done.12), channel_id=1, source_target_pairs={{4,0},{8,4},{12,8},{16,12},{20,16},{24,20},{28,24},{5,1},{9,5},{13... | collective-permute-start | bytes 1572872 | tf_op jit(solution)/shard_map/ppermute | solution.py:16
  88.1 26.3 %collective-permute-start.10 = (bf16[256,1024]{1,0:T(8,128)(2,1)S(1)}, bf16[256,1024]{1,0:T(8,128)(2,1)S(1)}, u32[]{:S(2)}, u32[]{:S(2)}) collective-permute-start(bf16[256,1024]{1,0:T(8,128)(2,1)S(1)} %collective-permute-done.9), channel_id=1, source_target_pairs={{0,4},{4,8},{8,12},{12,16},{16,20},{20,24},{24,28},{1,5},{5,9},{9,... | collective-permute-start | bytes 1572872 | tf_op jit(solution)/shard_map/ppermute | solution.py:16
  93.0 26.4 %collective-permute-start.14 = (bf16[256,1024]{1,0:T(8,128)(2,1)S(1)}, bf16[256,1024]{1,0:T(8,128)(2,1)S(1)}, u32[]{:S(2)}, u32[]{:S(2)}) collective-permute-start(bf16[256,1024]{1,0:T(8,128)(2,1)S(1)} %collective-permute-done.13), channel_id=1, source_target_pairs={{4,0},{8,4},{12,8},{16,12},{20,16},{24,20},{28,24},{5,1},{9,5},{13... | collective-permute-start | bytes 1572872 | tf_op jit(solution)/shard_map/ppermute | solution.py:16
  114.4 25.4 %collective-permute-start.11 = (bf16[256,1024]{1,0:T(8,128)(2,1)S(1)}, bf16[256,1024]{1,0:T(8,128)(2,1)S(1)}, u32[]{:S(2)}, u32[]{:S(2)}) collective-permute-start(bf16[256,1024]{1,0:T(8,128)(2,1)S(1)} %collective-permute-done.10), channel_id=1, source_target_pairs={{0,4},{4,8},{8,12},{12,16},{16,20},{20,24},{24,28},{1,5},{5,9},{9,... | collective-permute-start | bytes 1572872 | tf_op jit(solution)/shard_map/ppermute | solution.py:16
  119.3 20.7 %copy-start.2 = (bf16[256,1024]{1,0:T(8,128)(2,1)S(1)}, bf16[256,1024]{1,0:T(8,128)(2,1)}, u32[]{:S(2)}) copy-start(bf16[256,1024]{1,0:T(8,128)(2,1)} %param.3) | copy-start | bytes 1572868
  119.4 20.8 %collective-permute-start.15 = (bf16[256,1024]{1,0:T(8,128)(2,1)S(1)}, bf16[256,1024]{1,0:T(8,128)(2,1)S(1)}, u32[]{:S(2)}, u32[]{:S(2)}) collective-permute-start(bf16[256,1024]{1,0:T(8,128)(2,1)S(1)} %collective-permute-done.14), channel_id=1, source_target_pairs={{4,0},{8,4},{12,8},{16,12},{20,16},{24,20},{28,24},{5,1},{9,5},{13... | collective-permute-start | bytes 1572872 | tf_op jit(solution)/shard_map/ppermute | solution.py:16
  145.1 0.7 copy-start.3
  217.7 0.9 copy-start.1
Sparse Core Ops, SparseCore 0:
  145.2 64.3 all-gather.2
